TPU v7x, 32 devices: a whole 2x2x4 slice. The times are simulated.
32 devices in a mesh: rep: 4 (over y, core), ep: 8 (over z, x).
Axes of the slice: x: 2, y: 2, z: 4, core: 2. Of those that a mesh axis runs over, the one named last changes fastest.
Arguments:
- tokens: bfloat16 [8192, 2048], P(('rep', 'ep')), may hold values from -6 to 6
- expert_ids: int32 [8192, 8], P(('rep', 'ep')), may hold values from 0 to 127, as said below
- gate_weights: float32 [8192, 8], P(('rep', 'ep')), may hold values from 0.25 to 1
- w_gate: bfloat16 [8, 768, 2048], P('ep'), may hold values from -0.125 to 0.125
- w_up: bfloat16 [8, 768, 2048], P('ep'), may hold values from -0.125 to 0.125
- w_down: bfloat16 [8, 768, 2048], P('ep'), may hold values from -0.21875 to 0.21875
- out_grad: bfloat16 [8192, 2048], P(('rep', 'ep')), may hold values from -6 to 6
Outputs:
- layer_out: bfloat16 [8192, 2048], P(('rep', 'ep'))
- tokens_grad: bfloat16 [8192, 2048], P(('rep', 'ep'))
- gates_grad: float32 [8192, 8], P(('rep', 'ep'))
- gate_w_grad: bfloat16 [8, 768, 2048], P('ep', 'rep')
- up_w_grad: bfloat16 [8, 768, 2048], P('ep', 'rep')
- down_w_grad: bfloat16 [8, 768, 2048], P('ep', 'rep')
Inputs may be any that keep to these rules, and one draw needn't show every extreme that they name: `expert_ids`: entry j of a row lies in [16 * j, 16 * j + 16); in the rows of one device no id below 8 appears more than 32 times, and some id below 8 appears exactly 32 times.
All inputs are finite; a program needn't handle non-finite values.
Results may differ from a plain program's by a relative error of at most 0.0065.
Values may be sent and summed in bfloat16 or wider, within the bound.
No kernel may reach another device: no remote copies, remote signals or barrier semaphores. Data moves between devices by JAX's collectives and lax.ppermute only.
A program may use at most 128 MiB of HBM per device.

v0:
```python
import jax
import jax.numpy as jnp
from jax import lax
from jax.sharding import PartitionSpec as P

STRIPE = 16


def silu_grad(value):
    sigmoid_value = jax.nn.sigmoid(value)
    return sigmoid_value * (1.0 + value * (1.0 - sigmoid_value))


def rows_times(left, right):
    return lax.dot_general(
        left, right, (((1,), (1,)), ((), ())), preferred_element_type=jnp.float32
    )


def inner_rows(left, right):
    return lax.dot_general(
        left, right, (((0,), (0,)), ((), ())), preferred_element_type=jnp.float32
    )


def matmul(left, right):
    return jnp.dot(left, right, preferred_element_type=jnp.float32)


def body(tokens, expert_ids, gate_weights, w_gate, w_up, w_down, out_grad):
    tok_count, feature_width = tokens.shape
    top_count = expert_ids.shape[1]
    experts = lax.axis_size("ep")
    per_pair = tok_count // 8
    total_slots = experts * per_pair
    live_cols = min(top_count, -(-experts // STRIPE))
    assigned = tok_count * live_cols
    flat_ids = expert_ids[:, :live_cols].reshape(-1)
    flat_gates = gate_weights[:, :live_cols].reshape(-1)
    live_mask = flat_ids < experts
    onehot = flat_ids[:, None] == jnp.arange(experts, dtype=jnp.int32)[None, :]
    position = jnp.arange(assigned, dtype=jnp.int32)
    earlier = (position[:, None] > position[None, :]).astype(jnp.bfloat16)
    before = matmul(earlier, onehot.astype(jnp.bfloat16))
    slot_rank = jnp.sum(jnp.where(onehot, before, 0.0), axis=1).astype(jnp.int32)
    slot_index = jnp.where(live_mask, flat_ids * per_pair + slot_rank, -1)
    slot_ids = jnp.arange(total_slots, dtype=jnp.int32)
    hit = slot_ids[:, None] == slot_index[None, :]
    slot_gate = jnp.sum(jnp.where(hit, flat_gates[None, :], 0.0), axis=1)
    pick = jnp.any(hit.reshape(total_slots, tok_count, live_cols), axis=2).astype(jnp.bfloat16)
    send_rows = matmul(pick, tokens).astype(jnp.bfloat16)
    grad_rows = matmul(pick, out_grad)
    scaled_grad = (slot_gate[:, None] * grad_rows).astype(jnp.bfloat16)

    def exchange(rows):
        return lax.all_to_all(
            rows.reshape(experts, per_pair, feature_width),
            "ep",
            split_axis=0,
            concat_axis=0,
            tiled=True,
        ).reshape(total_slots, feature_width)

    rows_in = exchange(send_rows)
    grad_in = exchange(scaled_grad)
    copies = lax.axis_size("rep")
    by_pieces = copies == 4

    def to_copy(values, step):
        return lax.ppermute(values, "rep", [(r, r ^ step) for r in range(copies)])

    if by_pieces:
        far_rows = to_copy(rows_in, 2)
        near_rows = to_copy(rows_in, 1)
    else:
        gathered_rows = lax.all_gather(rows_in, "rep", axis=0, tiled=True)
        gathered_grad = lax.all_gather(grad_in, "rep", axis=0, tiled=True)
    gate_mat = w_gate[0]
    up_mat = w_up[0]
    down_mat = w_down[0]
    gate_up_mat = jnp.concatenate([gate_mat, up_mat], axis=0)
    hidden_units = gate_mat.shape[0]
    pre_both_own = rows_times(rows_in, gate_up_mat)
    pre_gate = pre_both_own[:, :hidden_units]
    pre_up = pre_both_own[:, hidden_units:]
    activated = jax.nn.silu(pre_gate)
    hidden = (activated * pre_up).astype(jnp.bfloat16)
    expert_out = matmul(hidden, down_mat).astype(jnp.bfloat16)
    expert_out, grad_in = lax.optimization_barrier((expert_out, grad_in))
    returned = lax.all_to_all(
        expert_out.reshape(experts, per_pair, feature_width),
        "ep",
        split_axis=0,
        concat_axis=0,
        tiled=True,
    ).reshape(total_slots, feature_width)
    hidden_grad = rows_times(grad_in, down_mat)
    gate_pre_grad = (hidden_grad * pre_up * silu_grad(pre_gate)).astype(jnp.bfloat16)
    up_pre_grad = (hidden_grad * activated).astype(jnp.bfloat16)
    token_part = matmul(jnp.concatenate([gate_pre_grad, up_pre_grad], axis=1), gate_up_mat).astype(
        jnp.bfloat16
    )
    if by_pieces:
        token_part, grad_out = lax.optimization_barrier((token_part, grad_in))
        far_grad = to_copy(grad_out, 2)
        near_grad = to_copy(grad_out, 1)
    part_back = lax.all_to_all(
        token_part.reshape(experts, per_pair, feature_width),
        "ep",
        split_axis=0,
        concat_axis=0,
        tiled=True,
    ).reshape(total_slots, feature_width)
    if by_pieces:
        returned, near_rows, near_grad = lax.optimization_barrier((returned, near_rows, near_grad))
    slot_grid = slot_index.reshape(tok_count, live_cols)
    gate_grid = flat_gates.reshape(tok_count, live_cols)
    layer_sum = jnp.zeros((tok_count, feature_width), jnp.float32)
    gate_cols = []
    back_pick = jnp.zeros((tok_count, total_slots), jnp.bfloat16)
    for col in range(live_cols):
        col_pick = (slot_grid[:, col : col + 1] == slot_ids[None, :]).astype(jnp.bfloat16)
        back_pick = back_pick + col_pick
        out_rows = matmul(col_pick, returned)
        layer_sum = layer_sum + gate_grid[:, col : col + 1] * out_rows
        gate_cols.append(jnp.sum(out_grad.astype(jnp.float32) * out_rows, axis=1))
    if by_pieces:
        layer_sum, far_rows, far_grad = lax.optimization_barrier((layer_sum, far_rows, far_grad))
        pieces = [
            (rows_in, grad_in),
            (near_rows, near_grad),
            (far_rows, far_grad),
            (to_copy(far_rows, 1), to_copy(far_grad, 1)),
        ]
    else:
        pieces = [(gathered_rows, gathered_grad)]
    layer_out = layer_sum.astype(jnp.bfloat16)
    gate_cols.extend([jnp.zeros((tok_count,), jnp.float32)] * (top_count - live_cols))
    gates_grad = jnp.stack(gate_cols, axis=1)
    share = gate_mat.shape[0] // copies
    start = lax.axis_index("rep") * share
    gate_share = lax.dynamic_slice_in_dim(gate_mat, start, share, axis=0)
    up_share = lax.dynamic_slice_in_dim(up_mat, start, share, axis=0)
    down_share = lax.dynamic_slice_in_dim(down_mat, start, share, axis=0)
    both_sum = None
    down_sum = None
    stacked_share = jnp.concatenate([gate_share, up_share], axis=0)
    for rows_p, grad_p in pieces:
        pre_both = rows_times(rows_p, stacked_share)
        pre_gate_s = pre_both[:, :share]
        pre_up_s = pre_both[:, share:]
        activated_s = jax.nn.silu(pre_gate_s)
        hidden_s = (activated_s * pre_up_s).astype(jnp.bfloat16)
        hidden_grad_s = rows_times(grad_p, down_share)
        gate_pre_grad_s = (hidden_grad_s * pre_up_s * silu_grad(pre_gate_s)).astype(jnp.bfloat16)
        up_pre_grad_s = (hidden_grad_s * activated_s).astype(jnp.bfloat16)
        both_p = inner_rows(jnp.concatenate([gate_pre_grad_s, up_pre_grad_s], axis=1), rows_p)
        down_p = inner_rows(hidden_s, grad_p)
        both_sum = both_p if both_sum is None else both_sum + both_p
        down_sum = down_p if down_sum is None else down_sum + down_p
    gate_w_grad = both_sum[:share].astype(jnp.bfloat16)[None]
    up_w_grad = both_sum[share:].astype(jnp.bfloat16)[None]
    down_w_grad = down_sum.astype(jnp.bfloat16)[None]
    part_back, gate_w_grad, up_w_grad, down_w_grad = lax.optimization_barrier(
        (part_back, gate_w_grad, up_w_grad, down_w_grad)
    )
    tokens_grad = matmul(back_pick, part_back).astype(jnp.bfloat16)
    return (layer_out, tokens_grad, gates_grad, gate_w_grad, up_w_grad, down_w_grad)


def solution(mesh):
    return jax.shard_map(
        body,
        mesh=mesh,
        in_specs=(
            P(("rep", "ep"), None),
            P(("rep", "ep"), None),
            P(("rep", "ep"), None),
            P("ep", None, None),
            P("ep", None, None),
            P("ep", None, None),
            P(("rep", "ep"), None),
        ),
        out_specs=(
            P(("rep", "ep"), None),
            P(("rep", "ep"), None),
            P(("rep", "ep"), None),
            P("ep", "rep", None),
            P("ep", "rep", None),
            P("ep", "rep", None),
        ),
        check_vma=False,
    )
```

profile of v0, /device:TPU:0, one launch (start us, length us, event | category | flops | bytes accessed | tf_op | source)
XLA Modules:
  0.0 129.3 jit_solution(9352168649783690748)
XLA Ops:
  1.7 2.6 %convolution_convert_fusion.1 = bf16[256,2048]{1,0:T(8,128)(2,1)} fusion(bf16[256,2048]{1,0:T(8,128)(2,1)} %param.7, s32[256]{0:T(256)S(1)} %compare_select_fusion.1), kind=kOutput, calls=%fused_computation.14 | convolution fusion | flops 269025280 | bytes 2098176 | tf_op jit(solution)/shard_map/dot_general | solution.py:27
  4.4 7.3 %all-to-all-start = ((bf16[8,32,2048]{2,1,0:T(8,128)(2,1)}), bf16[8,32,2048]{2,1,0:T(8,128)(2,1)}, u32[]{:S(2)}, u32[]{:S(2)}) async-start(bf16[8,32,2048]{2,1,0:T(8,128)(2,1)} %bitcast.75), calls=%async_computation | async-start | bytes 2097152 | tf_op jit(solution)/shard_map/all_to_all | solution.py:56
  12.4 2.6 %fusion.6 = bf16[256,2048]{1,0:T(8,128)(2,1)} fusion(bf16[256,2048]{1,0:T(8,128)(2,1)} %param.13, f32[256]{0:T(256)S(1)} %select_reduce_fusion, s32[256]{0:T(256)S(1)} %compare_select_fusion.1), kind=kOutput, calls=%fused_computation.11 | convolution fusion | flops 269549568 | bytes 2099200 | tf_op jit(solution)/shard_map/dot_general | solution.py:27
  15.1 22.4 %all-to-all-done = bf16[8,32,2048]{2,1,0:T(8,128)(2,1)} async-done(((bf16[8,32,2048]{2,1,0:T(8,128)(2,1)}), bf16[8,32,2048]{2,1,0:T(8,128)(2,1)}, u32[]{:S(2)}, u32[]{:S(2)}) %all-to-all-start) | async-done | bytes 1048608 | tf_op jit(solution)/shard_map/all_to_all | solution.py:56
  37.5 4.3 %all-to-all-start.1 = ((bf16[8,32,2048]{2,1,0:T(8,128)(2,1)}), bf16[8,32,2048]{2,1,0:T(8,128)(2,1)}, u32[]{:S(2)}, u32[]{:S(2)}) async-start(bf16[8,32,2048]{2,1,0:T(8,128)(2,1)} %bitcast.74), calls=%async_computation.1 | async-start | bytes 2097152 | tf_op jit(solution)/shard_map/all_to_all | solution.py:56
  42.9 2.8 %dynamic-slice_bitcast_fusion = (bf16[192,2048]{1,0:T(8,128)(2,1)}, bf16[192,2048]{1,0:T(8,128)(2,1)}) fusion(bf16[1,768,2048]{2,1,0:T(8,128)(2,1)} %param.11, s32[]{:T(128)S(6)} %select_n.28, bf16[1,768,2048]{2,1,0:T(8,128)(2,1)} %param.10), kind=kLoop, calls=%fused_computation.37 | loop fusion | bytes 3145732 | tf_op jit(solution)/shard_map/dynamic_slice | solution.py:143
  47.2 4.0 %fusion.1 = f32[256,1536]{1,0:T(8,128)S(1)} fusion(bf16[256,2048]{1,0:T(8,128)(2,1)} %bitcast.5, bf16[768,2048]{1,0:T(8,128)(2,1)S(1)} %bitcast.78, bf16[768,2048]{1,0:T(8,128)(2,1)} %bitcast.80), kind=kOutput, calls=%fused_computation.2 | convolution fusion | flops 1623195648 | bytes 8912896 | tf_op jit(solution)/shard_map/dot_general | solution.py:15
  52.4 2.0 %fusion.9 = bf16[256,2048]{1,0:T(8,128)(2,1)} fusion(bf16[1,768,2048]{2,1,0:T(8,128)(2,1)S(1)} %copy-done, f32[256,1536]{1,0:T(8,128)S(1)} %fusion.1), kind=kOutput, calls=%fused_computation.16 | convolution fusion | flops 807010304 | bytes 5767168 | tf_op jit(solution)/shard_map/dot_general | solution.py:27
  54.4 12.9 %all-to-all-done.1 = bf16[8,32,2048]{2,1,0:T(8,128)(2,1)} async-done(((bf16[8,32,2048]{2,1,0:T(8,128)(2,1)}), bf16[8,32,2048]{2,1,0:T(8,128)(2,1)}, u32[]{:S(2)}, u32[]{:S(2)}) %all-to-all-start.1) | async-done | bytes 1048608 | tf_op jit(solution)/shard_map/all_to_all | solution.py:56
  67.3 4.2 %all-to-all-start.2 = ((bf16[8,32,2048]{2,1,0:T(8,128)(2,1)}), bf16[8,32,2048]{2,1,0:T(8,128)(2,1)}, u32[]{:S(2)}, u32[]{:S(2)}) async-start(bf16[8,32,2048]{2,1,0:T(8,128)(2,1)} %bitcast.77), calls=%async_computation.2 | async-start | bytes 2097152 | tf_op jit(solution)/shard_map/all_to_all | solution.py:90
  71.6 3.0 %multiply_convert_fusion.1 = (bf16[256,768]{1,0:T(8,128)(2,1)S(1)}, bf16[256,768]{1,0:T(8,128)(2,1)S(1)}) fusion(f32[256,1536]{1,0:T(8,128)} %copy-done.11, bf16[256,2048]{1,0:T(8,128)(2,1)} %bitcast.10, bf16[1,768,2048]{2,1,0:T(8,128)(2,1)S(1)} %copy-done), kind=kOutput, calls=%fused_computation.40 | convolution fusion | flops 807862272 | bytes 6553600 | tf_op jit(solution)/shard_map/dot_general | solution.py:15
  75.2 2.8 %fusion.7 = bf16[256,2048]{1,0:T(8,128)(2,1)} fusion(bf16[768,2048]{1,0:T(8,128)(2,1)S(1)} %bitcast.79, bf16[768,2048]{1,0:T(8,128)(2,1)S(1)} %bitcast.81, bf16[256,768]{1,0:T(8,128)(2,1)S(1)} %get-tuple-element.35, bf16[256,768]{1,0:T(8,128)(2,1)S(1)} %get-tuple-element.34), kind=kOutput, calls=%fused_computation.12 | convolution fusion | flops 1625292800 | bytes 8126464 | tf_op jit(solution)/shard_map/dot_general | solution.py:27
  79.6 1.8 %fusion.84 = f32[256,384]{0,1:T(8,128)S(1)} fusion(bf16[256,2048]{1,0:T(8,128)(2,1)} %bitcast.5, bf16[192,2048]{1,0:T(8,128)(2,1)S(1)} %copy-done.4, bf16[192,2048]{1,0:T(8,128)(2,1)S(1)} %copy-done.6), kind=kOutput, calls=%fused_computation.118 | convolution fusion | flops 405798912 | bytes 3014656 | tf_op jit(solution)/shard_map/dot_general | solution.py:15
  83.2 2.8 %fusion.58 = f32[192,2048]{1,0:T(8,128)} fusion(bf16[256,2048]{1,0:T(8,128)(2,1)} %bitcast.10, f32[256,384]{0,1:T(8,128)S(1)} %fusion.84), kind=kOutput, calls=%fused_computation.93 | convolution fusion | flops 201621504 | bytes 3014656 | tf_op jit(solution)/shard_map/dot_general | solution.py:21
  85.9 3.4 %fusion.32 = f32[384,2048]{1,0:T(8,128)} fusion(bf16[256,2048]{1,0:T(8,128)(2,1)} %bitcast.5, bf16[256,192]{0,1:T(8,128)(2,1)S(1)} %get-tuple-element.43, bf16[256,192]{0,1:T(8,128)(2,1)S(1)} %get-tuple-element.42), kind=kOutput, calls=%fused_computation.53 | convolution fusion | flops 403046400 | bytes 4390912 | tf_op jit(solution)/shard_map/dot_general | solution.py:21
  89.4 7.6 %all-to-all-done.2 = bf16[8,32,2048]{2,1,0:T(8,128)(2,1)} async-done(((bf16[8,32,2048]{2,1,0:T(8,128)(2,1)}), bf16[8,32,2048]{2,1,0:T(8,128)(2,1)}, u32[]{:S(2)}, u32[]{:S(2)}) %all-to-all-start.2) | async-done | bytes 1048608 | tf_op jit(solution)/shard_map/all_to_all | solution.py:90
  97.0 4.4 %all-to-all-start.3 = ((bf16[8,32,2048]{2,1,0:T(8,128)(2,1)}), bf16[8,32,2048]{2,1,0:T(8,128)(2,1)}, u32[]{:S(2)}, u32[]{:S(2)}) async-start(bf16[8,32,2048]{2,1,0:T(8,128)(2,1)} %bitcast.76), calls=%async_computation.3 | async-start | bytes 2097152 | tf_op jit(solution)/shard_map/all_to_all | solution.py:107
  101.5 2.8 %broadcast_multiply_fusion = (bf16[256,2048]{1,0:T(8,128)(2,1)}, f32[256,2048]{1,0:T(8,128)S(1)}) fusion(f32[256]{0:T(256)S(1)} %bitcast.85, bf16[256,2048]{1,0:T(8,128)(2,1)} %bitcast.12, s32[256]{0:T(256)S(1)} %bitcast.82), kind=kOutput, calls=%fused_computation.23 | convolution fusion | flops 269549568 | bytes 4196352 | tf_op jit(solution)/shard_map/dot_general | solution.py:27
  104.3 1.8 %fusion.82 = f32[256,384]{0,1:T(8,128)S(1)} fusion(bf16[256,2048]{1,0:T(8,128)(2,1)} %collective-permute-done.2, bf16[192,2048]{1,0:T(8,128)(2,1)S(1)} %copy-done.5, bf16[192,2048]{1,0:T(8,128)(2,1)S(1)} %copy-done.7), kind=kOutput, calls=%fused_computation.116 | convolution fusion | flops 405798912 | bytes 3014656 | tf_op jit(solution)/shard_map/dot_general | solution.py:15
  106.2 1.8 %fusion.83 = f32[256,384]{0,1:T(8,128)S(1)} fusion(bf16[256,2048]{1,0:T(8,128)(2,1)} %collective-permute-done, bf16[192,2048]{1,0:T(8,128)(2,1)S(1)} %copy-done.5, bf16[192,2048]{1,0:T(8,128)(2,1)S(1)} %copy-done.7), kind=kOutput, calls=%fused_computation.117 | convolution fusion | flops 405798912 | bytes 3014656 | tf_op jit(solution)/shard_map/dot_general | solution.py:15
  110.3 1.8 %multiply_convert_fusion.13 = (bf16[256,192]{0,1:T(8,128)(2,1)S(1)}, bf16[256,192]{0,1:T(8,128)(2,1)S(1)}) fusion(f32[256,384]{0,1:T(8,128)S(1)} %fusion.83, bf16[256,2048]{1,0:T(8,128)(2,1)} %collective-permute-done.1, bf16[1,768,2048]{2,1,0:T(8,128)(2,1)S(1)} %copy-done, s32[]{:T(128)S(6)} %select_n.28), kind=kOutput, calls=%fused_computation.82 | convolution fusion | flops 201965568 | bytes 2424836 | tf_op jit(solution)/shard_map/dot_general | solution.py:15
  120.0 2.7 %fusion.13 = bf16[1,192,2048]{2,1,0:T(8,128)(2,1)} fusion(f32[192,2048]{1,0:T(8,128)S(1)} %fusion.59, f32[192,2048]{1,0:T(8,128)S(1)} %convolution_add_fusion.1, bf16[256,2048]{1,0:T(8,128)(2,1)} %collective-permute-done.3, f32[256,384]{0,1:T(8,128)S(1)} %fusion.82), kind=kOutput, calls=%fused_computation.18 | convolution fusion | flops 202801152 | bytes 5373952 | tf_op jit(solution)/shard_map/dot_general | solution.py:21
  124.5 2.1 %all-to-all-done.3 = bf16[8,32,2048]{2,1,0:T(8,128)(2,1)} async-done(((bf16[8,32,2048]{2,1,0:T(8,128)(2,1)}), bf16[8,32,2048]{2,1,0:T(8,128)(2,1)}, u32[]{:S(2)}, u32[]{:S(2)}) %all-to-all-start.3) | async-done | bytes 1048608 | tf_op jit(solution)/shard_map/all_to_all | solution.py:107
  126.6 2.7 %convolution_convert_fusion = bf16[256,2048]{1,0:T(8,128)(2,1)} fusion(bf16[256,2048]{1,0:T(8,128)(2,1)} %bitcast.14, s32[256]{0:T(256)S(1)} %bitcast.83), kind=kOutput, calls=%fused_computation.13 | convolution fusion | flops 269025280 | bytes 2098176 | tf_op jit(solution)/shard_map/dot_general | solution.py:27
  (60 shorter events, 21.5 us)
Async XLA Ops:
  0.6 51.8 %copy-start = (bf16[1,768,2048]{2,1,0:T(8,128)(2,1)S(1)}, bf16[1,768,2048]{2,1,0:T(8,128)(2,1)}, u32[]{:S(2)}) copy-start(bf16[1,768,2048]{2,1,0:T(8,128)(2,1)} %param.12) | copy-start | bytes 9437188
  4.4 33.1 %all-to-all-start = ((bf16[8,32,2048]{2,1,0:T(8,128)(2,1)}), bf16[8,32,2048]{2,1,0:T(8,128)(2,1)}, u32[]{:S(2)}, u32[]{:S(2)}) async-start(bf16[8,32,2048]{2,1,0:T(8,128)(2,1)} %bitcast.75), calls=%async_computation | async-start | bytes 2097152 | tf_op jit(solution)/shard_map/all_to_all | solution.py:56
  37.5 29.9 %all-to-all-start.1 = ((bf16[8,32,2048]{2,1,0:T(8,128)(2,1)}), bf16[8,32,2048]{2,1,0:T(8,128)(2,1)}, u32[]{:S(2)}, u32[]{:S(2)}) async-start(bf16[8,32,2048]{2,1,0:T(8,128)(2,1)} %bitcast.74), calls=%async_computation.1 | async-start | bytes 2097152 | tf_op jit(solution)/shard_map/all_to_all | solution.py:56
  42.0 5.2 %copy-start.8 = (bf16[1,768,2048]{2,1,0:T(8,128)(2,1)S(1)}, bf16[1,768,2048]{2,1,0:T(8,128)(2,1)}, u32[]{:S(2)}) copy-start(bf16[1,768,2048]{2,1,0:T(8,128)(2,1)} %param.11) | copy-start | bytes 9437188
  45.7 58.6 %collective-permute-start.2 = (bf16[256,2048]{1,0:T(8,128)(2,1)}, bf16[256,2048]{1,0:T(8,128)(2,1)}, u32[]{:S(2)}, u32[]{:S(2)}) collective-permute-start(bf16[256,2048]{1,0:T(8,128)(2,1)} %bitcast.5), channel_id=1, source_target_pairs={{0,16},{8,24},{16,0},{24,8},{1,17},{9,25},{17,1},{25,9},{2,18},{10... | collective-permute-start | bytes 3145736 | tf_op jit(solution)/shard_map/ppermute | solution.py:70
  47.2 54.3 %collective-permute-start = (bf16[256,2048]{1,0:T(8,128)(2,1)}, bf16[256,2048]{1,0:T(8,128)(2,1)}, u32[]{:S(2)}, u32[]{:S(2)}) collective-permute-start(bf16[256,2048]{1,0:T(8,128)(2,1)} %bitcast.5), channel_id=1, source_target_pairs={{0,8},{8,0},{16,24},{24,16},{1,9},{9,1},{17,25},{25,17},{2,10},{10... | collective-permute-start | bytes 3145736 | tf_op jit(solution)/shard_map/ppermute | solution.py:70
  51.2 1.2 copy-start.11
  67.3 29.6 %all-to-all-start.2 = ((bf16[8,32,2048]{2,1,0:T(8,128)(2,1)}), bf16[8,32,2048]{2,1,0:T(8,128)(2,1)}, u32[]{:S(2)}, u32[]{:S(2)}) async-start(bf16[8,32,2048]{2,1,0:T(8,128)(2,1)} %bitcast.77), calls=%async_computation.2 | async-start | bytes 2097152 | tf_op jit(solution)/shard_map/all_to_all | solution.py:90
  71.6 3.1 %copy-start.9 = (bf16[1,768,2048]{2,1,0:T(8,128)(2,1)S(1)}, bf16[1,768,2048]{2,1,0:T(8,128)(2,1)}, u32[]{:S(2)}) copy-start(bf16[1,768,2048]{2,1,0:T(8,128)(2,1)} %param.11) | copy-start | bytes 9437188
  71.6 3.6 %copy-start.10 = (bf16[1,768,2048]{2,1,0:T(8,128)(2,1)S(1)}, bf16[1,768,2048]{2,1,0:T(8,128)(2,1)}, u32[]{:S(2)}) copy-start(bf16[1,768,2048]{2,1,0:T(8,128)(2,1)} %param.10) | copy-start | bytes 9437188
  75.2 4.3 %copy-start.4 = (bf16[192,2048]{1,0:T(8,128)(2,1)S(1)}, bf16[192,2048]{1,0:T(8,128)(2,1)}, u32[]{:S(2)}) copy-start(bf16[192,2048]{1,0:T(8,128)(2,1)} %get-tuple-element.48) | copy-start | bytes 2359300
  75.2 4.3 %copy-start.6 = (bf16[192,2048]{1,0:T(8,128)(2,1)S(1)}, bf16[192,2048]{1,0:T(8,128)(2,1)}, u32[]{:S(2)}) copy-start(bf16[192,2048]{1,0:T(8,128)(2,1)} %get-tuple-element.49) | copy-start | bytes 2359300
  78.1 26.2 %collective-permute-start.3 = (bf16[256,2048]{1,0:T(8,128)(2,1)}, bf16[256,2048]{1,0:T(8,128)(2,1)}, u32[]{:S(2)}, u32[]{:S(2)}) collective-permute-start(bf16[256,2048]{1,0:T(8,128)(2,1)} %bitcast.10), channel_id=1, source_target_pairs={{0,16},{8,24},{16,0},{24,8},{1,17},{9,25},{17,1},{25,9},{2,18},{10... | collective-permute-start | bytes 3145736 | tf_op jit(solution)/shard_map/ppermute | solution.py:70
  79.6 21.9 %collective-permute-start.1 = (bf16[256,2048]{1,0:T(8,128)(2,1)}, bf16[256,2048]{1,0:T(8,128)(2,1)}, u32[]{:S(2)}, u32[]{:S(2)}) collective-permute-start(bf16[256,2048]{1,0:T(8,128)(2,1)} %bitcast.10), channel_id=1, source_target_pairs={{0,8},{8,0},{16,24},{24,16},{1,9},{9,1},{17,25},{25,17},{2,10},{10... | collective-permute-start | bytes 3145736 | tf_op jit(solution)/shard_map/ppermute | solution.py:70
  97.0 29.6 %all-to-all-start.3 = ((bf16[8,32,2048]{2,1,0:T(8,128)(2,1)}), bf16[8,32,2048]{2,1,0:T(8,128)(2,1)}, u32[]{:S(2)}, u32[]{:S(2)}) async-start(bf16[8,32,2048]{2,1,0:T(8,128)(2,1)} %bitcast.76), calls=%async_computation.3 | async-start | bytes 2097152 | tf_op jit(solution)/shard_map/all_to_all | solution.py:107
  101.4 2.9 %copy-start.5 = (bf16[192,2048]{1,0:T(8,128)(2,1)S(1)}, bf16[192,2048]{1,0:T(8,128)(2,1)}, u32[]{:S(2)}) copy-start(bf16[192,2048]{1,0:T(8,128)(2,1)} %get-tuple-element.48) | copy-start | bytes 2359300
  101.4 2.8 %copy-start.7 = (bf16[192,2048]{1,0:T(8,128)(2,1)S(1)}, bf16[192,2048]{1,0:T(8,128)(2,1)}, u32[]{:S(2)}) copy-start(bf16[192,2048]{1,0:T(8,128)(2,1)} %get-tuple-element.49) | copy-start | bytes 2359300
  106.1 12.3 %collective-permute-start.5 = (bf16[256,2048]{1,0:T(8,128)(2,1)}, bf16[256,2048]{1,0:T(8,128)(2,1)S(1)}, u32[]{:S(2)}, u32[]{:S(2)}) collective-permute-start(bf16[256,2048]{1,0:T(8,128)(2,1)} %collective-permute-done.2), channel_id=1, source_target_pairs={{0,8},{8,0},{16,24},{24,16},{1,9},{9,1},{17,25},{25,17},{2,10},{10... | collective-permute-start | bytes 3145736 | tf_op jit(solution)/shard_map/ppermute | solution.py:70
  108.0 11.0 %collective-permute-start.4 = (bf16[256,2048]{1,0:T(8,128)(2,1)}, bf16[256,2048]{1,0:T(8,128)(2,1)S(1)}, u32[]{:S(2)}, u32[]{:S(2)}) collective-permute-start(bf16[256,2048]{1,0:T(8,128)(2,1)} %collective-permute-done.3), channel_id=1, source_target_pairs={{0,8},{8,0},{16,24},{24,16},{1,9},{9,1},{17,25},{25,17},{2,10},{10... | collective-permute-start | bytes 3145736 | tf_op jit(solution)/shard_map/ppermute | solution.py:70
  110.3 3.7 %copy-start.3 = (bf16[256,2048]{1,0:T(8,128)(2,1)S(1)}, bf16[256,2048]{1,0:T(8,128)(2,1)}, u32[]{:S(2)}) copy-start(bf16[256,2048]{1,0:T(8,128)(2,1)} %param.13) | copy-start | bytes 3145732
  114.0 2.8 %copy-start.2 = (f32[192,2048]{1,0:T(8,128)S(1)}, f32[192,2048]{1,0:T(8,128)}, u32[]{:S(2)}) copy-start(f32[192,2048]{1,0:T(8,128)} %fusion.58) | copy-start | bytes 4718596
  120.0 2.7 %copy-start.1 = (f32[384,2048]{1,0:T(8,128)S(1)}, f32[384,2048]{1,0:T(8,128)}, u32[]{:S(2)}) copy-start(f32[384,2048]{1,0:T(8,128)} %fusion.32) | copy-start | bytes 9437188
where the time goes:
time: 130 us; the launch traced here: 129 us
  matrix products  49.9 us (38%)
  waiting for transfers between devices  45.1 us (35%)
  starting transfers between devices  23.8 us (18%)
  local copies, waits for them, and re-layouts  7.6 us (6%)
  other arithmetic  1.94 us (1%)
    all_to_all x2, waiting for transfers between devices, exchange(): lax.all_to_all(rows.reshape(experts, per_pair, feature_width), 'ep', spli...  35.4 us
    dot_general x10, matrix products, rows_times(): lax.dot_general(left, right, (((1,), (1,)), ((), ())), preferred_element_...  19 us
    dot_general x7, matrix products, matmul(): return jnp.dot(left, right, preferred_element_type=jnp.float32)  15.8 us
    dot_general x8, matrix products, inner_rows(): lax.dot_general(left, right, (((0,), (0,)), ((), ())), preferred_element_...  15.1 us
    all_to_all x2, starting transfers between devices, exchange(): lax.all_to_all(rows.reshape(experts, per_pair, feature_width), 'ep', spli...  11.5 us
    all_to_all x1, waiting for transfers between devices, body(): lax.all_to_all(expert_out.reshape(experts, per_pair, feature_width), 'ep'...  7.62 us
    all_to_all x1, starting transfers between devices, body(): lax.all_to_all(token_part.reshape(experts, per_pair, feature_width), 'ep'...  4.41 us
    all_to_all x1, starting transfers between devices, body(): lax.all_to_all(expert_out.reshape(experts, per_pair, feature_width), 'ep'...  4.24 us
  transfers between devices with their start and end apart: 10, of which 4 were waited for; matrix products, arithmetic and copies ran while one was open for 40% of the time, Pallas kernels for 0%

commit v1 on v0

--- a/solution.py
+++ b/solution.py
@@ -4,6 +4,29 @@
 from jax.sharding import PartitionSpec as P
 
 STRIPE = 16
+
+
+def in_blocks(x, dim, peers):
+    before, after = (x.shape[:dim], x.shape[dim + 1 :])
+    return jnp.moveaxis(x.reshape(*before, peers, -1, *after), dim, 0)
+
+
+def in_order(blocks, dim):
+    dims = list(blocks.shape[1:])
+    dims[dim] *= blocks.shape[0]
+    return jnp.moveaxis(blocks, 0, dim).reshape(dims)
+
+
+def exchange_directly(shard, axis, split_dim, concat_dim):
+    peers, place = (lax.axis_size(axis), lax.axis_index(axis))
+    parts = in_blocks(shard, split_dim, peers)
+    out = parts
+    for turn in range(1, peers):
+        target, source = ((place + turn) % peers, (place - turn) % peers)
+        sent = lax.dynamic_index_in_dim(parts, target, 0)
+        other = lax.ppermute(sent, axis, [(i, (i + turn) % peers) for i in range(peers)])
+        out = lax.dynamic_update_slice_in_dim(out, other, source, axis=0)
+    return in_order(out, concat_dim)
 
 
 def silu_grad(value):
@@ -87,12 +110,8 @@
     hidden = (activated * pre_up).astype(jnp.bfloat16)
     expert_out = matmul(hidden, down_mat).astype(jnp.bfloat16)
     expert_out, grad_in = lax.optimization_barrier((expert_out, grad_in))
-    returned = lax.all_to_all(
-        expert_out.reshape(experts, per_pair, feature_width),
-        "ep",
-        split_axis=0,
-        concat_axis=0,
-        tiled=True,
+    returned = exchange_directly(
+        expert_out.reshape(experts, per_pair, feature_width), "ep", 0, 0
     ).reshape(total_slots, feature_width)
     hidden_grad = rows_times(grad_in, down_mat)
     gate_pre_grad = (hidden_grad * pre_up * silu_grad(pre_gate)).astype(jnp.bfloat16)

time: 130 us -> 170 us (1.31)
  waiting for transfers between devices: 45.1 us -> 79 us
  starting transfers between devices: 23.8 us -> 32.5 us
  matrix products: 49.9 us -> 46.1 us
    ppermute x0 -> x7, waiting for transfers between devices: none -> 44 us  [exchange_directly(): lax.ppermute(sent, axis, [(i, (i + turn) % peers) for i in range(peers)])]
    ppermute x0 -> x7, starting transfers between devices: none -> 12.6 us  [exchange_directly(): lax.ppermute(sent, axis, [(i, (i + turn) % peers) for i in range(peers)])]
    all_to_all x1 -> x0, waiting for transfers between devices: 7.62 us -> none  [body(): lax.all_to_all(expert_out.reshape(experts, per_pair, feature_width), 'ep'...]
    all_to_all x1 -> x0, starting transfers between devices: 4.24 us -> none  [body(): lax.all_to_all(expert_out.reshape(experts, per_pair, feature_width), 'ep'...]
    dot_general x8, matrix products: 15.1 us -> 12.2 us  [inner_rows(): lax.dot_general(left, right, (((0,), (0,)), ((), ())), preferred_element_...]
    all_to_all x1, waiting for transfers between devices: 2.11 us -> 0.01 us  [body(): lax.all_to_all(token_part.reshape(experts, per_pair, feature_width), 'ep'...]
  transfers between devices with their start and end apart: 10 -> 16, of which waited for: 4 -> 8; matrix products, arithmetic and copies ran while one was open for 40% -> 29% of each run, Pallas kernels for 0% -> 0%
where the time goes in v1:
time: 170 us
  waiting for transfers between devices  79 us (46%)
  matrix products  46.1 us (27%)
  starting transfers between devices  32.5 us (19%)
  local copies, waits for them, and re-layouts  8.69 us (5%)
  other arithmetic  1.95 us (1%)
    ppermute x7, waiting for transfers between devices, exchange_directly(): lax.ppermute(sent, axis, [(i, (i + turn) % peers) for i in range(peers)])  44 us
    all_to_all x2, waiting for transfers between devices, exchange(): lax.all_to_all(rows.reshape(experts, per_pair, feature_width), 'ep', spli...  35.1 us
    dot_general x10, matrix products, rows_times(): lax.dot_general(left, right, (((1,), (1,)), ((), ())), preferred_element_...  19.5 us
    dot_general x7, matrix products, matmul(): return jnp.dot(left, right, preferred_element_type=jnp.float32)  14.4 us
    ppermute x7, starting transfers between devices, exchange_directly(): lax.ppermute(sent, axis, [(i, (i + turn) % peers) for i in range(peers)])  12.6 us
    dot_general x8, matrix products, inner_rows(): lax.dot_general(left, right, (((0,), (0,)), ((), ())), preferred_element_...  12.2 us
    all_to_all x2, starting transfers between devices, exchange(): lax.all_to_all(rows.reshape(experts, per_pair, feature_width), 'ep', spli...  11.5 us
    all_to_all x1, starting transfers between devices, body(): lax.all_to_all(token_part.reshape(experts, per_pair, feature_width), 'ep'...  4.79 us
  transfers between devices with their start and end apart: 16, of which 8 were waited for; matrix products, arithmetic and copies ran while one was open for 29% of the time, Pallas kernels for 0%

profile of v1, /device:TPU:0, one launch (start us, length us, event | category | flops | bytes accessed | tf_op | source)
XLA Modules:
  0.0 169.6 jit_solution(6034154104342461595)
XLA Ops:
  1.7 2.6 %convolution_convert_fusion.1 = bf16[256,2048]{1,0:T(8,128)(2,1)} fusion(bf16[256,2048]{1,0:T(8,128)(2,1)} %param.7, s32[256]{0:T(256)S(1)} %compare_select_fusion.1), kind=kOutput, calls=%fused_computation.14 | convolution fusion | flops 269025280 | bytes 2098176 | tf_op jit(solution)/shard_map/dot_general | solution.py:50
  4.4 7.3 %all-to-all-start = ((bf16[8,32,2048]{2,1,0:T(8,128)(2,1)}), bf16[8,32,2048]{2,1,0:T(8,128)(2,1)}, u32[]{:S(2)}, u32[]{:S(2)}) async-start(bf16[8,32,2048]{2,1,0:T(8,128)(2,1)} %bitcast.75), calls=%async_computation | async-start | bytes 2097152 | tf_op jit(solution)/shard_map/all_to_all | solution.py:79
  12.4 2.6 %fusion.6 = bf16[256,2048]{1,0:T(8,128)(2,1)} fusion(bf16[256,2048]{1,0:T(8,128)(2,1)} %param.13, f32[256]{0:T(256)S(1)} %select_reduce_fusion, s32[256]{0:T(256)S(1)} %compare_select_fusion.1), kind=kOutput, calls=%fused_computation.11 | convolution fusion | flops 269549568 | bytes 2099200 | tf_op jit(solution)/shard_map/dot_general | solution.py:50
  15.1 22.4 %all-to-all-done = bf16[8,32,2048]{2,1,0:T(8,128)(2,1)} async-done(((bf16[8,32,2048]{2,1,0:T(8,128)(2,1)}), bf16[8,32,2048]{2,1,0:T(8,128)(2,1)}, u32[]{:S(2)}, u32[]{:S(2)}) %all-to-all-start) | async-done | bytes 1048608 | tf_op jit(solution)/shard_map/all_to_all | solution.py:79
  37.5 4.2 %all-to-all-start.1 = ((bf16[8,32,2048]{2,1,0:T(8,128)(2,1)}), bf16[8,32,2048]{2,1,0:T(8,128)(2,1)}, u32[]{:S(2)}, u32[]{:S(2)}) async-start(bf16[8,32,2048]{2,1,0:T(8,128)(2,1)} %bitcast.74), calls=%async_computation.1 | async-start | bytes 2097152 | tf_op jit(solution)/shard_map/all_to_all | solution.py:79
  43.1 2.8 %dynamic-slice_bitcast_fusion = (bf16[192,2048]{1,0:T(8,128)(2,1)}, bf16[192,2048]{1,0:T(8,128)(2,1)}) fusion(bf16[1,768,2048]{2,1,0:T(8,128)(2,1)} %param.11, s32[]{:T(128)S(6)} %select_n.158, bf16[1,768,2048]{2,1,0:T(8,128)(2,1)} %param.10), kind=kLoop, calls=%fused_computation.37 | loop fusion | bytes 3145732 | tf_op jit(solution)/shard_map/dynamic_slice | solution.py:162
  47.4 4.0 %fusion.1 = f32[256,1536]{1,0:T(8,128)S(1)} fusion(bf16[256,2048]{1,0:T(8,128)(2,1)} %bitcast.5, bf16[768,2048]{1,0:T(8,128)(2,1)S(1)} %bitcast.80, bf16[768,2048]{1,0:T(8,128)(2,1)} %bitcast.82), kind=kOutput, calls=%fused_computation.2 | convolution fusion | flops 1623195648 | bytes 8912896 | tf_op jit(solution)/shard_map/dot_general | solution.py:38
  52.7 2.0 %fusion.9 = bf16[256,2048]{1,0:T(8,128)(2,1)} fusion(bf16[1,768,2048]{2,1,0:T(8,128)(2,1)S(1)} %copy-done, f32[256,1536]{1,0:T(8,128)S(1)} %fusion.1), kind=kOutput, calls=%fused_computation.16 | convolution fusion | flops 807010304 | bytes 5767168 | tf_op jit(solution)/shard_map/dot_general | solution.py:50
  54.7 12.6 %all-to-all-done.1 = bf16[8,32,2048]{2,1,0:T(8,128)(2,1)} async-done(((bf16[8,32,2048]{2,1,0:T(8,128)(2,1)}), bf16[8,32,2048]{2,1,0:T(8,128)(2,1)}, u32[]{:S(2)}, u32[]{:S(2)}) %all-to-all-start.1) | async-done | bytes 1048608 | tf_op jit(solution)/shard_map/all_to_all | solution.py:79
  67.3 3.0 %multiply_convert_fusion.1 = (bf16[256,768]{1,0:T(8,128)(2,1)S(1)}, bf16[256,768]{1,0:T(8,128)(2,1)S(1)}) fusion(f32[256,1536]{1,0:T(8,128)} %copy-done.8, bf16[256,2048]{1,0:T(8,128)(2,1)} %bitcast.10, bf16[1,768,2048]{2,1,0:T(8,128)(2,1)S(1)} %copy-done), kind=kOutput, calls=%fused_computation.40 | convolution fusion | flops 807862272 | bytes 6553600 | tf_op jit(solution)/shard_map/dot_general | solution.py:38
  71.0 2.8 %fusion.7 = bf16[256,2048]{1,0:T(8,128)(2,1)} fusion(bf16[768,2048]{1,0:T(8,128)(2,1)S(1)} %bitcast.81, bf16[768,2048]{1,0:T(8,128)(2,1)S(1)} %bitcast.83, bf16[256,768]{1,0:T(8,128)(2,1)S(1)} %get-tuple-element.35, bf16[256,768]{1,0:T(8,128)(2,1)S(1)} %get-tuple-element.34), kind=kOutput, calls=%fused_computation.12 | convolution fusion | flops 1625292800 | bytes 8126464 | tf_op jit(solution)/shard_map/dot_general | solution.py:50
  77.5 4.8 %all-to-all-start.2 = ((bf16[8,32,2048]{2,1,0:T(8,128)(2,1)}), bf16[8,32,2048]{2,1,0:T(8,128)(2,1)}, u32[]{:S(2)}, u32[]{:S(2)}) async-start(bf16[8,32,2048]{2,1,0:T(8,128)(2,1)} %bitcast.79), calls=%async_computation.2 | async-start | bytes 2097152 | tf_op jit(solution)/shard_map/all_to_all | solution.py:126
  82.2 2.3 %fusion.84 = f32[256,384]{0,1:T(8,128)S(1)} fusion(bf16[256,2048]{1,0:T(8,128)(2,1)} %bitcast.5, bf16[192,2048]{1,0:T(8,128)(2,1)} %get-tuple-element.55, bf16[192,2048]{1,0:T(8,128)(2,1)} %get-tuple-element.56), kind=kOutput, calls=%fused_computation.132 | convolution fusion | flops 405798912 | bytes 3014656 | tf_op jit(solution)/shard_map/dot_general | solution.py:38
  88.3 2.1 %collective-permute-start.1 = (bf16[1,1,32,2048]{3,2,0,1:T(8,128)(2,1)S(1)}, bf16[1,1,32,2048]{3,2,0,1:T(8,128)(2,1)S(1)}, u32[]{:S(2)}, u32[]{:S(2)}) collective-permute-start(bf16[1,1,32,2048]{3,2,0,1:T(8,128)(2,1)S(1)} %get-tuple-element.43), channel_id=1, source_target_pairs={{0,2},{1,3},{2,4},{3,5},{4,6},{5,7},{6,0},{7,1},{8,10},{9,11},{10,... | collective-permute-start | bytes 393224 | tf_op jit(solution)/shard_map/ppermute | solution.py:27
  92.0 14.6 %collective-permute-done.1 = bf16[1,1,32,2048]{3,2,0,1:T(8,128)(2,1)S(1)} collective-permute-done((bf16[1,1,32,2048]{3,2,0,1:T(8,128)(2,1)S(1)}, bf16[1,1,32,2048]{3,2,0,1:T(8,128)(2,1)S(1)}, u32[]{:S(2)}, u32[]{:S(2)}) %collective-permute-start.1) | collective-permute-done | bytes 131104 | tf_op jit(solution)/shard_map/ppermute | solution.py:27
  106.6 4.1 %collective-permute-start.2 = (bf16[1,1,32,2048]{3,2,0,1:T(8,128)(2,1)S(1)}, bf16[1,1,32,2048]{3,2,0,1:T(8,128)(2,1)S(1)}, u32[]{:S(2)}, u32[]{:S(2)}) collective-permute-start(bf16[1,1,32,2048]{3,2,0,1:T(8,128)(2,1)S(1)} %get-tuple-element.42), channel_id=1, source_target_pairs={{0,3},{1,4},{2,5},{3,6},{4,7},{5,0},{6,1},{7,2},{8,11},{9,12},{10,... | collective-permute-start | bytes 393224 | tf_op jit(solution)/shard_map/ppermute | solution.py:27
  110.8 8.4 %collective-permute-done.2 = bf16[1,1,32,2048]{3,2,0,1:T(8,128)(2,1)S(1)} collective-permute-done((bf16[1,1,32,2048]{3,2,0,1:T(8,128)(2,1)S(1)}, bf16[1,1,32,2048]{3,2,0,1:T(8,128)(2,1)S(1)}, u32[]{:S(2)}, u32[]{:S(2)}) %collective-permute-start.2) | collective-permute-done | bytes 131104 | tf_op jit(solution)/shard_map/ppermute | solution.py:27
  119.3 7.7 %collective-permute-done.3 = bf16[1,1,32,2048]{3,2,0,1:T(8,128)(2,1)S(1)} collective-permute-done((bf16[1,1,32,2048]{3,2,0,1:T(8,128)(2,1)S(1)}, bf16[1,1,32,2048]{3,2,0,1:T(8,128)(2,1)S(1)}, u32[]{:S(2)}, u32[]{:S(2)}) %collective-permute-start.3) | collective-permute-done | bytes 131104 | tf_op jit(solution)/shard_map/ppermute | solution.py:27
  127.0 5.8 %collective-permute-done.4 = bf16[1,1,32,2048]{3,2,0,1:T(8,128)(2,1)S(1)} collective-permute-done((bf16[1,1,32,2048]{3,2,0,1:T(8,128)(2,1)S(1)}, bf16[1,1,32,2048]{3,2,0,1:T(8,128)(2,1)S(1)}, u32[]{:S(2)}, u32[]{:S(2)}) %collective-permute-start.4) | collective-permute-done | bytes 131104 | tf_op jit(solution)/shard_map/ppermute | solution.py:27
  132.9 4.9 %collective-permute-done.5 = bf16[1,1,32,2048]{3,2,0,1:T(8,128)(2,1)S(1)} collective-permute-done((bf16[1,1,32,2048]{3,2,0,1:T(8,128)(2,1)S(1)}, bf16[1,1,32,2048]{3,2,0,1:T(8,128)(2,1)S(1)}, u32[]{:S(2)}, u32[]{:S(2)}) %collective-permute-start.5) | collective-permute-done | bytes 131104 | tf_op jit(solution)/shard_map/ppermute | solution.py:27
  137.8 5.0 %collective-permute-start.6 = (bf16[1,1,32,2048]{3,2,0,1:T(8,128)(2,1)S(1)}, bf16[1,1,32,2048]{3,2,0,1:T(8,128)(2,1)S(1)}, u32[]{:S(2)}, u32[]{:S(2)}) collective-permute-start(bf16[1,1,32,2048]{3,2,0,1:T(8,128)(2,1)S(1)} %get-tuple-element.38), channel_id=1, source_target_pairs={{0,7},{1,0},{2,1},{3,2},{4,3},{5,4},{6,5},{7,6},{8,15},{9,8},{10,9... | collective-permute-start | bytes 393224 | tf_op jit(solution)/shard_map/ppermute | solution.py:27
  142.8 2.5 %collective-permute-done.6 = bf16[1,1,32,2048]{3,2,0,1:T(8,128)(2,1)S(1)} collective-permute-done((bf16[1,1,32,2048]{3,2,0,1:T(8,128)(2,1)S(1)}, bf16[1,1,32,2048]{3,2,0,1:T(8,128)(2,1)S(1)}, u32[]{:S(2)}, u32[]{:S(2)}) %collective-permute-start.6) | collective-permute-done | bytes 131104 | tf_op jit(solution)/shard_map/ppermute | solution.py:27
  162.5 2.5 %fusion.13 = bf16[1,192,2048]{2,1,0:T(8,128)(2,1)} fusion(f32[192,2048]{1,0:T(8,128)S(1)} %fusion.59, f32[192,2048]{1,0:T(8,128)S(1)} %convolution_add_fusion.1, bf16[256,2048]{1,0:T(8,128)(2,1)} %collective-permute-done.10, f32[256,384]{0,1:T(8,128)S(1)} %fusion.82), kind=kOutput, calls=%fused_computation.18 | convolution fusion | flops 202801152 | bytes 5373952 | tf_op jit(solution)/shard_map/dot_general | solution.py:44
  166.9 2.7 %convolution_convert_fusion = bf16[256,2048]{1,0:T(8,128)(2,1)} fusion(bf16[256,2048]{1,0:T(8,128)(2,1)} %bitcast.14, s32[256]{0:T(256)S(1)} %bitcast.85), kind=kOutput, calls=%fused_computation.13 | convolution fusion | flops 269025280 | bytes 2098176 | tf_op jit(solution)/shard_map/dot_general | solution.py:50
  (74 shorter events, 34.4 us)
Async XLA Ops:
  0.6 52.0 %copy-start = (bf16[1,768,2048]{2,1,0:T(8,128)(2,1)S(1)}, bf16[1,768,2048]{2,1,0:T(8,128)(2,1)}, u32[]{:S(2)}) copy-start(bf16[1,768,2048]{2,1,0:T(8,128)(2,1)} %param.12) | copy-start | bytes 9437188
  4.4 33.1 %all-to-all-start = ((bf16[8,32,2048]{2,1,0:T(8,128)(2,1)}), bf16[8,32,2048]{2,1,0:T(8,128)(2,1)}, u32[]{:S(2)}, u32[]{:S(2)}) async-start(bf16[8,32,2048]{2,1,0:T(8,128)(2,1)} %bitcast.75), calls=%async_computation | async-start | bytes 2097152 | tf_op jit(solution)/shard_map/all_to_all | solution.py:79
  37.5 29.9 %all-to-all-start.1 = ((bf16[8,32,2048]{2,1,0:T(8,128)(2,1)}), bf16[8,32,2048]{2,1,0:T(8,128)(2,1)}, u32[]{:S(2)}, u32[]{:S(2)}) async-start(bf16[8,32,2048]{2,1,0:T(8,128)(2,1)} %bitcast.74), calls=%async_computation.1 | async-start | bytes 2097152 | tf_op jit(solution)/shard_map/all_to_all | solution.py:79
  42.3 5.2 %copy-start.5 = (bf16[1,768,2048]{2,1,0:T(8,128)(2,1)S(1)}, bf16[1,768,2048]{2,1,0:T(8,128)(2,1)}, u32[]{:S(2)}) copy-start(bf16[1,768,2048]{2,1,0:T(8,128)(2,1)} %param.11) | copy-start | bytes 9437188
  45.9 100.9 %collective-permute-start.9 = (bf16[256,2048]{1,0:T(8,128)(2,1)}, bf16[256,2048]{1,0:T(8,128)(2,1)}, u32[]{:S(2)}, u32[]{:S(2)}) collective-permute-start(bf16[256,2048]{1,0:T(8,128)(2,1)} %bitcast.5), channel_id=1, source_target_pairs={{0,16},{8,24},{16,0},{24,8},{1,17},{9,25},{17,1},{25,9},{2,18},{10... | collective-permute-start | bytes 3145736 | tf_op jit(solution)/shard_map/ppermute | solution.py:93
  47.4 97.9 %collective-permute-start.7 = (bf16[256,2048]{1,0:T(8,128)(2,1)}, bf16[256,2048]{1,0:T(8,128)(2,1)}, u32[]{:S(2)}, u32[]{:S(2)}) collective-permute-start(bf16[256,2048]{1,0:T(8,128)(2,1)} %bitcast.5), channel_id=1, source_target_pairs={{0,8},{8,0},{16,24},{24,16},{1,9},{9,1},{17,25},{25,17},{2,10},{10... | collective-permute-start | bytes 3145736 | tf_op jit(solution)/shard_map/ppermute | solution.py:93
  67.3 3.0 %copy-start.6 = (bf16[1,768,2048]{2,1,0:T(8,128)(2,1)S(1)}, bf16[1,768,2048]{2,1,0:T(8,128)(2,1)}, u32[]{:S(2)}) copy-start(bf16[1,768,2048]{2,1,0:T(8,128)(2,1)} %param.11) | copy-start | bytes 9437188
  67.3 3.6 %copy-start.7 = (bf16[1,768,2048]{2,1,0:T(8,128)(2,1)S(1)}, bf16[1,768,2048]{2,1,0:T(8,128)(2,1)}, u32[]{:S(2)}) copy-start(bf16[1,768,2048]{2,1,0:T(8,128)(2,1)} %param.10) | copy-start | bytes 9437188
  73.8 73.1 %collective-permute-start.10 = (bf16[256,2048]{1,0:T(8,128)(2,1)}, bf16[256,2048]{1,0:T(8,128)(2,1)}, u32[]{:S(2)}, u32[]{:S(2)}) collective-permute-start(bf16[256,2048]{1,0:T(8,128)(2,1)} %bitcast.10), channel_id=1, source_target_pairs={{0,16},{8,24},{16,0},{24,8},{1,17},{9,25},{17,1},{25,9},{2,18},{10... | collective-permute-start | bytes 3145736 | tf_op jit(solution)/shard_map/ppermute | solution.py:93
  75.3 70.1 %collective-permute-start.8 = (bf16[256,2048]{1,0:T(8,128)(2,1)}, bf16[256,2048]{1,0:T(8,128)(2,1)}, u32[]{:S(2)}, u32[]{:S(2)}) collective-permute-start(bf16[256,2048]{1,0:T(8,128)(2,1)} %bitcast.10), channel_id=1, source_target_pairs={{0,8},{8,0},{16,24},{24,16},{1,9},{9,1},{17,25},{25,17},{2,10},{10... | collective-permute-start | bytes 3145736 | tf_op jit(solution)/shard_map/ppermute | solution.py:93
  76.2 12.0 %collective-permute-start = (bf16[1,1,32,2048]{3,2,0,1:T(8,128)(2,1)S(1)}, bf16[1,1,32,2048]{3,2,0,1:T(8,128)(2,1)S(1)}, u32[]{:S(2)}, u32[]{:S(2)}) collective-permute-start(bf16[1,1,32,2048]{3,2,0,1:T(8,128)(2,1)S(1)} %constant_dynamic-slice_fusion.6), channel_id=1, source_target_pairs={{0,1},{1,2},{2,3},{3,4},{4,5},{5,6},{6,7},{7,0},{8,9},{9,10},{10,1... | collective-permute-start | bytes 393224 | tf_op jit(solution)/shard_map/ppermute | solution.py:27
  77.5 89.5 %all-to-all-start.2 = ((bf16[8,32,2048]{2,1,0:T(8,128)(2,1)}), bf16[8,32,2048]{2,1,0:T(8,128)(2,1)}, u32[]{:S(2)}, u32[]{:S(2)}) async-start(bf16[8,32,2048]{2,1,0:T(8,128)(2,1)} %bitcast.79), calls=%async_computation.2 | async-start | bytes 2097152 | tf_op jit(solution)/shard_map/all_to_all | solution.py:126
  84.5 3.7 %copy-start.2 = (bf16[256,2048]{1,0:T(8,128)(2,1)S(1)}, bf16[256,2048]{1,0:T(8,128)(2,1)}, u32[]{:S(2)}) copy-start(bf16[256,2048]{1,0:T(8,128)(2,1)} %fusion.9) | copy-start | bytes 3145732
  88.3 18.3 %collective-permute-start.1 = (bf16[1,1,32,2048]{3,2,0,1:T(8,128)(2,1)S(1)}, bf16[1,1,32,2048]{3,2,0,1:T(8,128)(2,1)S(1)}, u32[]{:S(2)}, u32[]{:S(2)}) collective-permute-start(bf16[1,1,32,2048]{3,2,0,1:T(8,128)(2,1)S(1)} %get-tuple-element.43), channel_id=1, source_target_pairs={{0,2},{1,3},{2,4},{3,5},{4,6},{5,7},{6,0},{7,1},{8,10},{9,11},{10,... | collective-permute-start | bytes 393224 | tf_op jit(solution)/shard_map/ppermute | solution.py:27
  92.0 54.8 %copy-start.3 = (bf16[192,2048]{1,0:T(8,128)(2,1)S(1)}, bf16[192,2048]{1,0:T(8,128)(2,1)}, u32[]{:S(2)}) copy-start(bf16[192,2048]{1,0:T(8,128)(2,1)} %get-tuple-element.55) | copy-start | bytes 2359300
  92.0 54.8 %copy-start.4 = (bf16[192,2048]{1,0:T(8,128)(2,1)S(1)}, bf16[192,2048]{1,0:T(8,128)(2,1)}, u32[]{:S(2)}) copy-start(bf16[192,2048]{1,0:T(8,128)(2,1)} %get-tuple-element.56) | copy-start | bytes 2359300
  106.6 12.5 %collective-permute-start.2 = (bf16[1,1,32,2048]{3,2,0,1:T(8,128)(2,1)S(1)}, bf16[1,1,32,2048]{3,2,0,1:T(8,128)(2,1)S(1)}, u32[]{:S(2)}, u32[]{:S(2)}) collective-permute-start(bf16[1,1,32,2048]{3,2,0,1:T(8,128)(2,1)S(1)} %get-tuple-element.42), channel_id=1, source_target_pairs={{0,3},{1,4},{2,5},{3,6},{4,7},{5,0},{6,1},{7,2},{8,11},{9,12},{10,... | collective-permute-start | bytes 393224 | tf_op jit(solution)/shard_map/ppermute | solution.py:27
  119.2 7.8 %collective-permute-start.3 = (bf16[1,1,32,2048]{3,2,0,1:T(8,128)(2,1)S(1)}, bf16[1,1,32,2048]{3,2,0,1:T(8,128)(2,1)S(1)}, u32[]{:S(2)}, u32[]{:S(2)}) collective-permute-start(bf16[1,1,32,2048]{3,2,0,1:T(8,128)(2,1)S(1)} %get-tuple-element.41), channel_id=1, source_target_pairs={{0,4},{1,5},{2,6},{3,7},{4,0},{5,1},{6,2},{7,3},{8,12},{9,13},{10,... | collective-permute-start | bytes 393224 | tf_op jit(solution)/shard_map/ppermute | solution.py:27
  127.0 5.9 %collective-permute-start.4 = (bf16[1,1,32,2048]{3,2,0,1:T(8,128)(2,1)S(1)}, bf16[1,1,32,2048]{3,2,0,1:T(8,128)(2,1)S(1)}, u32[]{:S(2)}, u32[]{:S(2)}) collective-permute-start(bf16[1,1,32,2048]{3,2,0,1:T(8,128)(2,1)S(1)} %get-tuple-element.40), channel_id=1, source_target_pairs={{0,5},{1,6},{2,7},{3,0},{4,1},{5,2},{6,3},{7,4},{8,13},{9,14},{10,... | collective-permute-start | bytes 393224 | tf_op jit(solution)/shard_map/ppermute | solution.py:27
  132.9 5.0 %collective-permute-start.5 = (bf16[1,1,32,2048]{3,2,0,1:T(8,128)(2,1)S(1)}, bf16[1,1,32,2048]{3,2,0,1:T(8,128)(2,1)S(1)}, u32[]{:S(2)}, u32[]{:S(2)}) collective-permute-start(bf16[1,1,32,2048]{3,2,0,1:T(8,128)(2,1)S(1)} %get-tuple-element.39), channel_id=1, source_target_pairs={{0,6},{1,7},{2,0},{3,1},{4,2},{5,3},{6,4},{7,5},{8,14},{9,15},{10,... | collective-permute-start | bytes 393224 | tf_op jit(solution)/shard_map/ppermute | solution.py:27
  137.8 7.5 %collective-permute-start.6 = (bf16[1,1,32,2048]{3,2,0,1:T(8,128)(2,1)S(1)}, bf16[1,1,32,2048]{3,2,0,1:T(8,128)(2,1)S(1)}, u32[]{:S(2)}, u32[]{:S(2)}) collective-permute-start(bf16[1,1,32,2048]{3,2,0,1:T(8,128)(2,1)S(1)} %get-tuple-element.38), channel_id=1, source_target_pairs={{0,7},{1,0},{2,1},{3,2},{4,3},{5,4},{6,5},{7,6},{8,15},{9,8},{10,9... | collective-permute-start | bytes 393224 | tf_op jit(solution)/shard_map/ppermute | solution.py:27
  148.7 12.3 %collective-permute-start.12 = (bf16[256,2048]{1,0:T(8,128)(2,1)}, bf16[256,2048]{1,0:T(8,128)(2,1)S(1)}, u32[]{:S(2)}, u32[]{:S(2)}) collective-permute-start(bf16[256,2048]{1,0:T(8,128)(2,1)} %collective-permute-done.9), channel_id=1, source_target_pairs={{0,8},{8,0},{16,24},{24,16},{1,9},{9,1},{17,25},{25,17},{2,10},{10... | collective-permute-start | bytes 3145736 | tf_op jit(solution)/shard_map/ppermute | solution.py:93
  150.6 11.0 %collective-permute-start.11 = (bf16[256,2048]{1,0:T(8,128)(2,1)}, bf16[256,2048]{1,0:T(8,128)(2,1)S(1)}, u32[]{:S(2)}, u32[]{:S(2)}) collective-permute-start(bf16[256,2048]{1,0:T(8,128)(2,1)} %collective-permute-done.10), channel_id=1, source_target_pairs={{0,8},{8,0},{16,24},{24,16},{1,9},{9,1},{17,25},{25,17},{2,10},{10... | collective-permute-start | bytes 3145736 | tf_op jit(solution)/shard_map/ppermute | solution.py:93
  152.9 3.6 %copy-start.1 = (bf16[256,2048]{1,0:T(8,128)(2,1)S(1)}, bf16[256,2048]{1,0:T(8,128)(2,1)}, u32[]{:S(2)}) copy-start(bf16[256,2048]{1,0:T(8,128)(2,1)} %param.13) | copy-start | bytes 3145732
  (1 other events, 1.2 us)
